TPU v7x, 256 devices: a whole 4x4x8 slice. The times are simulated.
256 devices in a mesh: group: 32 (over x, z_lo, core), tp: 8 (over y, z_hi).
Axes of the slice: x: 4, y: 4, z: 8 (z_hi: 2, z_lo: 4; z = z_hi * 4 + z_lo), core: 2. Of those that a mesh axis runs over, the one named last changes fastest.
Arguments:
- prefill_x: bfloat16 [16384, 4096], P('group', 'tp'), may hold values from -6 to 6
- decode_x: bfloat16 [128, 4096], P('group', 'tp'), may hold values from -6 to 6
- ln_gain: float32 [4096], replicated, may hold values from 0.1 to 1.9
- ln_bias: float32 [4096], replicated, may hold values from -3 to 3
- qkv_weight: bfloat16 [4096, 3, 2048], P(None, None, 'tp'), may hold values from -0.09375 to 0.09375
- qkv_bias: float32 [3, 2048], P(None, 'tp'), may hold values from -3 to 3
- prior_cache: bfloat16 [32, 2, 512, 2048], P('group', None, None, 'tp'), may hold values from -144 to 144, as said below
- prefill_offset: int32 [32], P('group'), may hold values from 0 to 512, as said below
- home_cache: bfloat16 [128, 2, 256, 2048], P('group', None, None, 'tp'), may hold values from -144 to 144, as said below
- piece_len: int32 [128, 3], P('group'), may hold values from 0 to 1024, as said below
- side_store: bfloat16 [256, 2, 1024, 2048], P('group', None, None, 'tp'), may hold values from -144 to 144, as said below
Outputs:
- prefill_out: bfloat16 [16384, 2048], P('group', 'tp')
- decode_out: bfloat16 [128, 2048], P('group', 'tp')
Inputs may be any that keep to these rules, and one draw needn't show every extreme that they name: `prior_cache`: keys already rotated. `prefill_offset`: the largest value, 512, and 0 occur in every draw. `home_cache`: keys already rotated. `piece_len`: columns 0 and 2 are at most 1024 and reach it in every draw, 0 meaning no piece on that side; column 1 is 1 to 256 and reaches 256 in every draw. `side_store`: keys already rotated.
All inputs are finite; a program needn't handle non-finite values.
Results may differ from a plain program's by a relative error of at most 0.019.
The roundings to bfloat16 on the way count: a program that leaves them out, or rounds other values in their place, can miss the bound.
Values may be sent and summed in bfloat16 or wider, within the bound.
No kernel may reach another device: no remote copies, remote signals or barrier semaphores. Data moves between devices by JAX's collectives and lax.ppermute only.
A program may use at most 128 MiB of HBM per device.

v0:
```python
from functools import reduce
import math
import jax
import jax.numpy as jnp
from jax import lax
from jax.sharding import PartitionSpec as P

HD = 128
ROT = 32
EPS = 1e-05
NEG = -1e30


def with_halo(block, sides, width):
    for axis, dim in sides:
        count = lax.axis_size(axis)
        forward = [(i, i + 1) for i in range(count - 1)]
        forward.append((count - 1, 0))
        backward = [(target, source) for source, target in forward]
        low = lax.ppermute(
            lax.slice_in_dim(block, block.shape[dim] - width, None, axis=dim), axis, forward
        )
        high = lax.ppermute(lax.slice_in_dim(block, 0, width, axis=dim), axis, backward)
        block = jnp.concatenate([low, block, high], axis=dim)
    return block


def layer_norm(rows, gain, shift):
    rows = rows.astype(jnp.float32)
    middle = jnp.mean(rows, axis=-1, keepdims=True)
    centred = rows - middle
    spread = jnp.mean(centred * centred, axis=-1, keepdims=True)
    return (centred * lax.rsqrt(spread + EPS) * gain + shift).astype(jnp.bfloat16)


def rotate(vectors, positions):
    half = ROT // 2
    steps = jnp.arange(half, dtype=jnp.float32) * (2.0 / ROT)
    frequency = jnp.exp(-math.log(10000.0) * steps)
    angle = positions.astype(jnp.float32)[:, None] * frequency[None, :]
    cosine = jnp.cos(angle)[:, None, :]
    sine = jnp.sin(angle)[:, None, :]
    first = vectors[..., :half]
    second = vectors[..., half:ROT]
    return jnp.concatenate(
        [first * cosine - second * sine, second * cosine + first * sine, vectors[..., ROT:]],
        axis=-1,
    )


def project(normed, weight, bias, positions):
    count = normed.shape[0]
    width = weight.shape[2]
    mixed = jnp.dot(
        normed, weight.reshape(weight.shape[0], 3 * width), preferred_element_type=jnp.float32
    )
    mixed = (mixed + bias.reshape(1, 3 * width)).reshape(count, 3, width // HD, HD)
    query = rotate(mixed[:, 0], positions).astype(jnp.bfloat16)
    fresh_key = rotate(mixed[:, 1], positions).astype(jnp.bfloat16)
    fresh_value = mixed[:, 2].astype(jnp.bfloat16)
    return (query, fresh_key, fresh_value)


def attend_rows(query, keys, values, live):
    scores = jnp.einsum("qhd,khd->hqk", query, keys, preferred_element_type=jnp.float32) * (
        1.0 / math.sqrt(HD)
    )
    masked = jnp.where(live[None], scores, NEG)
    highest = jnp.max(masked, axis=2, keepdims=True)
    weights = jnp.where(live[None], jnp.exp(masked - highest), 0.0)
    total = jnp.sum(weights, axis=2)
    mixed = jnp.einsum(
        "hqk,khd->qhd", weights.astype(jnp.bfloat16), values, preferred_element_type=jnp.float32
    )
    return (mixed / jnp.transpose(total)[:, :, None]).astype(jnp.bfloat16)


def prefill_attend(query, fresh_key, fresh_value, prior, offset):
    count, heads = (query.shape[0], query.shape[1])
    capacity = prior.shape[1]
    keys = jnp.concatenate([prior[0].reshape(capacity, heads, HD), fresh_key], axis=0)
    values = jnp.concatenate([prior[1].reshape(capacity, heads, HD), fresh_value], axis=0)
    block = min(count, 512)

    def one_block(start):
        places = start + jnp.arange(block, dtype=jnp.int32)
        live = jnp.concatenate(
            [
                jnp.broadcast_to(jnp.arange(capacity)[None, :] < offset, (block, capacity)),
                jnp.arange(count)[None, :] <= places[:, None],
            ],
            axis=1,
        )
        return attend_rows(query, keys, values, live)

    starts = jnp.arange(count // block, dtype=jnp.int32) * block
    return lax.map(one_block, starts).reshape(count, heads * HD)


def piece_partial(query, keys, values, live):
    scores = jnp.einsum("hd,khd->hk", query, keys, preferred_element_type=jnp.float32) * (
        1.0 / math.sqrt(HD)
    )
    masked = jnp.where(live[None], scores, NEG)
    highest = jnp.max(masked, axis=1)
    weights = jnp.where(live[None], jnp.exp(masked - highest[:, None]), 0.0)
    total = jnp.sum(weights, axis=1)
    summed = jnp.einsum(
        "hk,khd->hd", weights.astype(jnp.bfloat16), values, preferred_element_type=jnp.float32
    )
    return (highest, total, summed)


def piece_batch(query, store, lengths):
    count, capacity = (store.shape[0], store.shape[2])
    heads = query.shape[1]
    keys = store[:, 0].reshape(count, capacity, heads, HD)
    values = store[:, 1].reshape(count, capacity, heads, HD)
    live = jnp.arange(capacity)[None, :] < lengths[:, None]
    return jax.vmap(piece_partial)(query, keys, values, live)


def home_partial(query, fresh_key, fresh_value, cache, lengths):
    count, capacity = (cache.shape[0], cache.shape[2])
    heads = query.shape[1]
    keys = jnp.concatenate(
        [cache[:, 0].reshape(count, capacity, heads, HD), fresh_key[:, None]], axis=1
    )
    values = jnp.concatenate(
        [cache[:, 1].reshape(count, capacity, heads, HD), fresh_value[:, None]], axis=1
    )
    live = jnp.concatenate(
        [jnp.arange(capacity)[None, :] < lengths[:, None], jnp.ones((count, 1), jnp.bool_)], axis=1
    )
    return jax.vmap(piece_partial)(query, keys, values, live)


def combine(parts):
    highest = reduce(jnp.maximum, [part[0] for part in parts])
    factors = [jnp.exp(part[0] - highest) for part in parts]
    upper = reduce(jnp.add, [factor[:, :, None] * part[2] for factor, part in zip(factors, parts)])
    lower = reduce(jnp.add, [factor * part[1] for factor, part in zip(factors, parts)])
    return (upper / lower[:, :, None]).astype(jnp.bfloat16)


def local(
    prefill_x,
    decode_x,
    ln_gain,
    ln_bias,
    qkv_weight,
    qkv_bias,
    prior_cache,
    prefill_offset,
    home_cache,
    piece_len,
    side_store,
):
    count = prefill_x.shape[0]
    requests = decode_x.shape[0]
    rows = jnp.concatenate([prefill_x, decode_x], axis=0)
    partner = lax.ppermute(rows, "tz", [(0, 1), (1, 0)])
    own_y = lax.all_gather(rows, "ty", axis=1, tiled=True)
    partner_y = lax.all_gather(partner, "ty", axis=1, tiled=True)
    lower = lax.axis_index("tz") == 0
    first = jnp.where(lower, own_y, partner_y).reshape(rows.shape[0], -1, 1, rows.shape[1])
    second = jnp.where(lower, partner_y, own_y).reshape(rows.shape[0], -1, 1, rows.shape[1])
    whole = jnp.concatenate([first, second], axis=2).reshape(rows.shape[0], -1)
    normed = layer_norm(whole, ln_gain, ln_bias)
    positions = jnp.concatenate(
        [
            prefill_offset[0] + jnp.arange(count, dtype=jnp.int32),
            piece_len[:, 0] + piece_len[:, 1] + piece_len[:, 2],
        ],
        axis=0,
    )
    query, fresh_key, fresh_value = project(normed, qkv_weight, qkv_bias, positions)
    own_query = query[count:]
    home_parts = home_partial(
        own_query, fresh_key[count:], fresh_value[count:], home_cache, piece_len[:, 1]
    )
    groups = lax.axis_size("group")
    forward = [(i, (i + 1) % groups) for i in range(groups)]
    backward = [((i + 1) % groups, i) for i in range(groups)]
    heads = own_query.shape[1]

    def ask(lengths, pairs):
        packed = jnp.concatenate(
            [
                own_query.astype(jnp.float32).reshape(requests, -1),
                lengths[:, None].astype(jnp.float32),
            ],
            axis=1,
        )
        got = lax.ppermute(packed, "group", pairs)
        return (
            got[:, :-1].reshape(own_query.shape).astype(own_query.dtype),
            got[:, -1].astype(jnp.int32),
        )

    def answer(parts, pairs):
        highest, total, summed = parts
        packed = jnp.concatenate([summed, highest[:, :, None], total[:, :, None]], axis=2)
        got = lax.ppermute(packed, "group", pairs)
        return (got[:, :, HD], got[:, :, HD + 1], got[:, :, :HD])

    prev_query, prev_len = ask(piece_len[:, 2], forward)
    next_query, next_len = ask(piece_len[:, 0], backward)
    right_parts = answer(piece_batch(prev_query, side_store[:requests], prev_len), backward)
    left_parts = answer(piece_batch(next_query, side_store[requests:], next_len), forward)
    prefill_out = prefill_attend(
        query[:count], fresh_key[:count], fresh_value[:count], prior_cache[0], prefill_offset[0]
    )
    decode_out = combine([left_parts, home_parts, right_parts]).reshape(requests, -1)
    return (prefill_out, decode_out)


def solution(mesh):
    devices = mesh.devices.reshape(mesh.devices.shape[0], -1, 2)
    split = jax.sharding.Mesh(devices, ("group", "ty", "tz"))
    tp = ("ty", "tz")
    inner = jax.shard_map(
        local,
        mesh=split,
        in_specs=(
            P("group", tp),
            P("group", tp),
            P(),
            P(),
            P(None, None, tp),
            P(None, tp),
            P("group", None, None, tp),
            P("group"),
            P("group", None, None, tp),
            P("group", None),
            P("group", None, None, tp),
        ),
        out_specs=(P("group", tp), P("group", tp)),
        check_vma=False,
    )
    return inner
```

profile of v0, /device:TPU:8, one launch (start us, length us, event | category | flops | bytes accessed | tf_op | source)
XLA Modules:
  0.0 197.1 jit_solution(9359004009411949456)
XLA Ops:
  7.2 1.1 constant_dynamic-update-slice_fusion.1
  8.3 0.7 constant_dynamic-update-slice_fusion
  9.0 0.8 copy-done.1
  9.9 7.3 %collective-permute-start = (bf16[516,512]{1,0:T(8,128)(2,1)}, bf16[516,512]{1,0:T(8,128)(2,1)S(1)}, u32[]{:S(2)}, u32[]{:S(2)}) collective-permute-start(bf16[516,512]{1,0:T(8,128)(2,1)} %copy-done.1), channel_id=1, source_target_pairs={{0,1},{1,0},{2,3},{3,2},{4,5},{5,4},{6,7},{7,6},{8,9},{9,8},{10,11... | collective-permute-start | bytes 1585160 | tf_op jit(solution)/shard_map/ppermute | solution.py:162
  17.1 14.6 %collective-permute-done = bf16[516,512]{1,0:T(8,128)(2,1)S(1)} collective-permute-done((bf16[516,512]{1,0:T(8,128)(2,1)}, bf16[516,512]{1,0:T(8,128)(2,1)S(1)}, u32[]{:S(2)}, u32[]{:S(2)}) %collective-permute-start) | collective-permute-done | bytes 528416 | tf_op jit(solution)/shard_map/ppermute | solution.py:162
  31.7 0.8 copy-done.4
  32.5 0.7 add.81
  33.3 0.7 mul.188
  34.0 8.8 %copy.95 = bf16[4096,3,256]{0,2,1:T(8,128)(2,1)} copy(bf16[4096,3,256]{2,0,1:T(8,128)(2,1)} %param.15) | data formatting | bytes 12582912 | tf_op args[4]
  43.6 0.2 slice_convert_fusion.7
  43.8 0.2 multiply_cosine_fusion
  44.0 0.1 copy.99
  44.2 0.8 copy.98
  45.2 0.8 copy.102
  46.0 0.8 copy.92
  46.9 5.7 %fusion.76 = (bf16[4,1,1024,256]{3,2,1,0:T(8,128)(2,1)S(1)}, bf16[4,1,1024,256]{3,2,1,0:T(8,128)(2,1)}, bf16[4,1,1024,256]{3,2,1,0:T(8,128)(2,1)}, bf16[4,1,1024,256]{3,2,1,0:T(8,128)(2,1)}) fusion(bf16[8,2,1024,256]{3,2,1,0:T(8,128)(2,1)} %param.21), kind=kLoop, calls=%fused_computation.136 | loop fusion | bytes 16777216 | tf_op jit(solution)/shard_map/slice | solution.py:118
  52.6 4.0 %copy.126 = bf16[4,1,1024,256]{2,3,0,1:T(8,128)(2,1)} copy(bf16[4,1,1024,256]{3,2,1,0:T(8,128)(2,1)} %get-tuple-element.43) | data formatting | bytes 4194304 | tf_op jit(solution)/shard_map/reshape;squeeze | solution.py:117
  56.6 4.0 %reshape_squeeze.30 = bf16[4,1024,2,128]{3,2,1,0:T(2,128)(2,1)} reshape(bf16[4,1,1024,256]{3,2,1,0:T(8,128)(2,1)} %get-tuple-element.42) | data formatting | bytes 4194304 | tf_op jit(solution)/shard_map/reshape;squeeze | solution.py:118
  60.5 2.1 %fusion.78 = (bf16[4,1,256,256]{3,2,1,0:T(8,128)(2,1)S(1)}, bf16[4,1,256,256]{3,2,1,0:T(8,128)(2,1)}) fusion(bf16[4,2,256,256]{3,2,1,0:T(8,128)(2,1)} %param.19), kind=kLoop, calls=%fused_computation.138 | loop fusion | bytes 2097152 | tf_op jit(solution)/shard_map/slice | solution.py:127
  62.7 1.2 reshape_squeeze.31
  63.8 1.0 reshape_squeeze.28
  64.8 4.0 %copy.125 = bf16[4,1,1024,256]{2,3,0,1:T(8,128)(2,1)} copy(bf16[4,1,1024,256]{3,2,1,0:T(8,128)(2,1)} %get-tuple-element.41) | data formatting | bytes 4194304 | tf_op jit(solution)/shard_map/reshape;squeeze | solution.py:117
  68.8 2.1 %reshape_squeeze.27 = bf16[4,1024,2,128]{3,2,1,0:T(2,128)(2,1)} reshape(bf16[4,1,1024,256]{3,2,1,0:T(8,128)(2,1)S(1)} %get-tuple-element.40) | data formatting | bytes 4194304 | tf_op jit(solution)/shard_map/reshape;squeeze | solution.py:118
  71.1 1.0 pad_add_fusion
  72.1 9.0 %all-gather.5.cloned.1.call-done = bf16[516,2048]{1,0:T(8,128)(2,1)} async-done(((bf16[516,512]{1,0:T(8,128)(2,1)}), bf16[516,2048]{1,0:T(8,128)(2,1)}) %all-gather.5.cloned.1.call-update) | async-done | bytes 2113552 | tf_op jit(solution)/shard_map/all_gather | solution.py:164
  81.1 3.9 %broadcast_select_fusion.1 = (bf16[516,2048]{1,0:T(8,128)(2,1)S(1)}, bf16[516,2048]{1,0:T(8,128)(2,1)}) fusion(bf16[516,2048]{1,0:T(8,128)(2,1)} %all-gather.3.cloned.1.call-done, bf16[516,2048]{1,0:T(8,128)(2,1)} %all-gather.5.cloned.1.call-done, pred[]{:T(512)S(6)} %eq.3), kind=kLoop, calls=%fused_computation.14 | loop fusion | flops 2113536 | bytes 8454145 | tf_op jit(solution)/shard_map/jit(_where)/select_n | solution.py:166
  85.0 12.5 %reshape.299 = bf16[516,4,1,512]{3,2,1,0:T(2,128)(2,1)} reshape(bf16[516,2048]{1,0:T(8,128)(2,1)} %get-tuple-element.45) | data formatting | bytes 4227072 | tf_op jit(solution)/shard_map/reshape | solution.py:167
  97.5 5.4 %reshape.298 = bf16[516,4,1,512]{3,2,1,0:T(2,128)(2,1)} reshape(bf16[516,2048]{1,0:T(8,128)(2,1)S(1)} %get-tuple-element.44) | data formatting | bytes 4227072 | tf_op jit(solution)/shard_map/reshape | solution.py:166
  102.9 14.9 %convert_reduce_fusion = (f32[516]{0:T(1024)S(1)}, bf16[516,4,2,512]{3,2,1,0:T(2,128)(2,1)S(1)}) fusion(bf16[516,4,1,512]{3,2,1,0:T(2,128)(2,1)} %reshape.299, bf16[516,4,1,512]{3,2,1,0:T(2,128)(2,1)} %reshape.298), kind=kLoop, calls=%fused_computation.2 | loop fusion | flops 12680700 | bytes 8456208 | tf_op jit(solution)/shard_map/reduce_sum | solution.py:30
  117.8 6.1 %fusion.3 = f32[516]{0:T(1024)S(1)} fusion(bf16[516,4,2,512]{3,2,1,0:T(2,128)(2,1)S(1)} %get-tuple-element.39, f32[516]{0:T(1024)S(1)} %broadcast_multiply_fusion), kind=kLoop, calls=%fused_computation.5 | loop fusion | flops 8453628 | bytes 4231200 | tf_op jit(solution)/shard_map/reduce_sum | solution.py:32
  123.9 8.8 %fusion.6 = bf16[516,4,2,512]{3,2,1,0:T(2,128)(2,1)} fusion(bf16[516,4,2,512]{3,2,1,0:T(2,128)(2,1)S(1)} %get-tuple-element.39, f32[516]{0:T(1024)S(1)} %add_rsqrt_fusion, f32[516]{0:T(1024)S(1)} %broadcast_multiply_fusion, f32[4,2,512]{2,1,0:T(2,128)S(1)} %add.81, f32[4,2,512]{2,1,0:T(2,128)S(1)} %mul.188), kind=kLoop, calls=%fused_computation.8 | loop fusion | flops 12681216 | bytes 8491040 | tf_op jit(solution)/shard_map/convert_element_type | solution.py:33
  132.7 10.6 %convert_element_type.82 = bf16[516,4096]{1,0:T(8,128)(2,1)} reshape(bf16[516,4,2,512]{3,2,1,0:T(2,128)(2,1)} %fusion.6) | data formatting | bytes 8454144 | tf_op jit(solution)/shard_map/convert_element_type | solution.py:33
  143.3 8.8 %convolution_add_fusion = f32[516,768]{1,0:T(8,128)} fusion(bf16[516,4096]{1,0:T(8,128)(2,1)} %convert_element_type.82, bf16[4096,768]{0,1:T(8,128)(2,1)} %bitcast.118, f32[768]{0:T(1024)S(1)} %add.84), kind=kOutput, calls=%fused_computation.25 | convolution fusion | flops 3246787584 | bytes 12106752 | tf_op jit(solution)/shard_map/dot_general | solution.py:54
  152.1 2.1 %reshape.279 = f32[516,3,2,128]{3,2,1,0:T(2,128)S(1)} reshape(f32[516,768]{1,0:T(8,128)} %convolution_add_fusion) | data formatting | bytes 3170304 | tf_op jit(solution)/shard_map/reshape | solution.py:57
  154.2 0.4 fusion.77
  154.5 2.2 %copy.96 = bf16[516,3,2,128]{0,3,2,1:T(8,128)(2,1)} copy(f32[516,3,2,128]{3,2,1,0:T(2,128)S(1)} %reshape.279) | data formatting | bytes 2377728 | tf_op jit(solution)/shard_map/reshape | solution.py:57
  157.1 1.4 subtract_convert_fusion.1
  158.6 0.3 pad_maximum_fusion.3
  158.9 1.0 slice_bitcast_fusion
  160.0 0.8 slice.182
  160.8 0.3 pad_maximum_fusion.4
  161.4 5.7 %collective-permute-start.1 = (f32[4,257]{1,0:T(4,128)S(1)}, f32[4,257]{1,0:T(4,128)S(1)}, u32[]{:S(2)}, u32[]{:S(2)}) collective-permute-start(f32[4,257]{1,0:T(4,128)S(1)} %get-tuple-element.68), channel_id=1, source_target_pairs={{8,0},{16,8},{24,16},{32,24},{40,32},{48,40},{56,48},{64,56},{72,6... | collective-permute-start | bytes 12344 | tf_op jit(solution)/shard_map/ppermute | solution.py:195
  167.1 0.7 fusion.33
  167.8 2.4 %fusion.80 = (f32[2,512]{1,0:T(2,128)S(1)}, bf16[2,512,1024]{2,1,0:T(8,128)(2,1)S(1)}) fusion(f32[2,512,1024]{2,1,0:T(8,128)S(1)} %fusion.33, pred[512,1024]{1,0:T(8,128)(4,1)S(1)} %copy-done.5), kind=kOutput, calls=%fused_computation.140 | output fusion | flops 8389631 | bytes 6819840 | tf_op jit(solution)/shard_map/while/body/eval_jaxpr/sub | solution.py:70
  170.2 0.7 pad_maximum_fusion.2
  170.9 0.7 pad_maximum_fusion.1
  171.6 0.3 fusion.28
  171.9 0.8 fusion.23
  172.8 0.2 fusion.56
  173.2 2.0 %fusion.82 = f32[4,2,1,1024]{3,2,1,0:T(1,128)S(1)} fusion(bf16[4,2,128,1]{2,3,1,0:T(2,128)(2,1)S(1)} %reshape.303, bf16[4,1024,2,128]{1,3,2,0:T(8,128)(2,1)} %bitcast.117), kind=kOutput, calls=%fused_computation.142 | convolution fusion | flops 2097152 | bytes 2131968 | tf_op jit(solution)/shard_map/vmap(hd,khd->hk)/dot_general | solution.py:101
  175.2 0.2 fusion.50
  175.4 2.0 %fusion.8 = f32[4,2,1,128]{3,2,1,0:T(1,128)S(1)} fusion(bf16[4,1024,2,128]{3,2,1,0:T(2,128)(2,1)} %reshape_squeeze.30, bf16[4,2,1024,1]{2,0,1,3:T(4,128)(2,1)S(1)} %get-tuple-element.62), kind=kOutput, calls=%fused_computation.15 | convolution fusion | flops 2097152 | bytes 2117632 | tf_op jit(solution)/shard_map/vmap(hk,khd->hd)/dot_general | solution.py:108
  177.4 0.2 copy.121
  177.7 0.2 collective-permute-start.4
  178.1 0.4 fusion.81
  178.6 0.2 fusion.51
  178.8 2.0 %fusion.10 = f32[4,2,1,128]{3,2,1,0:T(1,128)S(1)} fusion(bf16[4,1024,2,128]{3,2,1,0:T(2,128)(2,1)} %reshape_squeeze.27, bf16[4,2,1024,1]{2,0,1,3:T(4,128)(2,1)S(1)} %get-tuple-element.60), kind=kOutput, calls=%fused_computation.17 | convolution fusion | flops 2097152 | bytes 2117632 | tf_op jit(solution)/shard_map/vmap(hk,khd->hd)/dot_general | solution.py:108
  180.8 0.2 copy.112
  181.0 0.5 collective-permute-start.2
  181.5 0.2 fusion.26
  181.7 0.9 copy.106
  182.5 0.2 copy.124
  182.7 6.7 %collective-permute-done.2 = f32[4,2,130]{0,1,2:T(2,128)S(1)} collective-permute-done((f32[4,2,130]{0,1,2:T(2,128)S(1)}, f32[4,2,130]{0,1,2:T(2,128)S(1)}, u32[]{:S(2)}, u32[]{:S(2)}) %collective-permute-start.2) | collective-permute-done | bytes 4192 | tf_op jit(solution)/shard_map/ppermute | solution.py:204
  189.6 0.7 copy.105
  (65 shorter events, 2.3 us)
Async XLA Ops:
  7.2 64.9 %all-gather.3.cloned.1.call-start = ((), (), s32[]{:S(2)}) async-start(), calls=%async_computation | async-start | bytes 2662400 | tf_op jit(solution)/shard_map/all_gather | solution.py:163
  9.0 0.8 copy-start.1
  9.8 71.3 %all-gather.5.cloned.1.call-start = ((), (), s32[]{:S(2)}) async-start(), calls=%async_computation.1 | async-start | bytes 2662400 | tf_op jit(solution)/shard_map/all_gather | solution.py:164
  9.9 21.8 %collective-permute-start = (bf16[516,512]{1,0:T(8,128)(2,1)}, bf16[516,512]{1,0:T(8,128)(2,1)S(1)}, u32[]{:S(2)}, u32[]{:S(2)}) collective-permute-start(bf16[516,512]{1,0:T(8,128)(2,1)} %copy-done.1), channel_id=1, source_target_pairs={{0,1},{1,0},{2,3},{3,2},{4,5},{5,4},{6,7},{7,6},{8,9},{9,8},{10,11... | collective-permute-start | bytes 1585160 | tf_op jit(solution)/shard_map/ppermute | solution.py:162
  31.7 0.8 copy-start.4
  34.0 8.9 %copy-start.9 = (f32[3,256]{1,0:T(4,128)S(1)}, f32[3,256]{1,0:T(4,128)}, u32[]{:S(2)}) copy-start(f32[3,256]{1,0:T(4,128)} %param.16) | copy-start | bytes 9220
  34.0 9.5 %copy-start.8 = (s32[4,3]{1,0:T(4,128)S(1)}, s32[4,3]{1,0:T(4,128)}, u32[]{:S(2)}) copy-start(s32[4,3]{1,0:T(4,128)} %param.20) | copy-start | bytes 148
  34.0 11.0 %copy-start.6 = (bf16[1,2,512,256]{3,2,1,0:T(8,128)(2,1)S(1)}, bf16[1,2,512,256]{3,2,1,0:T(8,128)(2,1)}, u32[]{:S(2)}) copy-start(bf16[1,2,512,256]{3,2,1,0:T(8,128)(2,1)} %param.17) | copy-start | bytes 1572868
  157.1 10.0 %copy-start.3 = (bf16[512,2,128]{2,0,1:T(8,128)(2,1)S(1)}, bf16[512,2,128]{2,0,1:T(8,128)(2,1)}, u32[]{:S(2)}) copy-start(bf16[512,2,128]{2,0,1:T(8,128)(2,1)} %copy.102) | copy-start | bytes 786436
  158.9 8.9 %copy-start.5 = (pred[512,1024]{1,0:T(8,128)(4,1)S(1)}, pred[512,1024]{1,0:T(8,128)(4,1)}, u32[]{:S(2)}) copy-start(pred[512,1024]{1,0:T(8,128)(4,1)} %pad_add_fusion) | copy-start | bytes 1572868
  161.2 11.8 %collective-permute-start.3 = (f32[4,257]{1,0:T(4,128)S(1)}, f32[4,257]{1,0:T(4,128)S(1)}, u32[]{:S(2)}, u32[]{:S(2)}) collective-permute-start(f32[4,257]{1,0:T(4,128)S(1)} %get-tuple-element.69), channel_id=1, source_target_pairs={{0,8},{8,16},{16,24},{24,32},{32,40},{40,48},{48,56},{56,64},{64,7... | collective-permute-start | bytes 12344 | tf_op jit(solution)/shard_map/ppermute | solution.py:195
  161.4 16.5 %collective-permute-start.1 = (f32[4,257]{1,0:T(4,128)S(1)}, f32[4,257]{1,0:T(4,128)S(1)}, u32[]{:S(2)}, u32[]{:S(2)}) collective-permute-start(f32[4,257]{1,0:T(4,128)S(1)} %get-tuple-element.68), channel_id=1, source_target_pairs={{8,0},{16,8},{24,16},{32,24},{40,32},{48,40},{56,48},{64,56},{72,6... | collective-permute-start | bytes 12344 | tf_op jit(solution)/shard_map/ppermute | solution.py:195
  167.8 3.1 %copy-start.2 = (bf16[4,256,2,128]{3,2,1,0:T(2,128)(2,1)S(1)}, bf16[4,256,2,128]{3,2,1,0:T(2,128)(2,1)}, u32[]{:S(2)}) copy-start(bf16[4,256,2,128]{3,2,1,0:T(2,128)(2,1)} %reshape_squeeze.28) | copy-start | bytes 1572868
  167.8 4.1 %copy-start.7 = (bf16[1,1,512,256]{2,3,1,0:T(8,128)(2,1)S(1)}, bf16[1,1,512,256]{2,3,1,0:T(8,128)(2,1)}, u32[]{:S(2)}) copy-start(bf16[1,1,512,256]{2,3,1,0:T(8,128)(2,1)} %copy.92) | copy-start | bytes 786436
  171.9 6.2 %copy-start = (bf16[4,1,1024,256]{2,3,0,1:T(8,128)(2,1)S(1)}, bf16[4,1,1024,256]{2,3,0,1:T(8,128)(2,1)}, u32[]{:S(2)}) copy-start(bf16[4,1,1024,256]{2,3,0,1:T(8,128)(2,1)} %copy.125) | copy-start | bytes 6291460
  177.7 5.0 %collective-permute-start.4 = (f32[4,2,130]{0,1,2:T(2,128)S(1)}, f32[4,2,130]{0,1,2:T(2,128)S(1)}, u32[]{:S(2)}, u32[]{:S(2)}) collective-permute-start(f32[4,2,130]{0,1,2:T(2,128)S(1)} %pad_maximum_fusion.6), channel_id=1, source_target_pairs={{8,0},{16,8},{24,16},{32,24},{40,32},{48,40},{56,48},{64,56},{72,6... | collective-permute-start | bytes 12488 | tf_op jit(solution)/shard_map/ppermute | solution.py:204
  181.0 8.4 %collective-permute-start.2 = (f32[4,2,130]{0,1,2:T(2,128)S(1)}, f32[4,2,130]{0,1,2:T(2,128)S(1)}, u32[]{:S(2)}, u32[]{:S(2)}) collective-permute-start(f32[4,2,130]{0,1,2:T(2,128)S(1)} %pad_maximum_fusion.5), channel_id=1, source_target_pairs={{0,8},{8,16},{16,24},{24,32},{32,40},{40,48},{48,56},{56,64},{64,7... | collective-permute-start | bytes 12488 | tf_op jit(solution)/shard_map/ppermute | solution.py:204
Sparse Core Ops, SparseCore 0:
  9.9 35.5 all-gather.2
  47.4 33.7 all-gather.4
where the time goes:
time: 199 us; the launch traced here: 197 us
  local copies, waits for them, and re-layouts  78.1 us (39%)
  other arithmetic  42.6 us (21%)
  waiting for transfers between devices  30.4 us (15%)
  matrix products  17.2 us (9%)
  between operations  15 us (8%)
  starting transfers between devices  13.8 us (7%)
    reduce_sum x1, other arithmetic, layer_norm(): middle = jnp.mean(rows, axis=-1, keepdims=True)  14.9 us
    ppermute x1, waiting for transfers between devices, local(): partner = lax.ppermute(rows, 'tz', [(0, 1), (1, 0)])  14.6 us
    unnamed x24, local copies, waits for them, and re-layouts  12.5 us
    reshape x1, local copies, waits for them, and re-layouts, local(): jnp.where(lower, partner_y, own_y)  12.5 us
    convert_element_type x1, local copies, waits for them, and re-layouts, layer_norm(): (centred * lax.rsqrt(spread + EPS) * gain + shift).astype(jnp.bfloat16)  10.6 us
    all_gather x1, waiting for transfers between devices, local(): partner_y = lax.all_gather(partner, 'ty', axis=1, tiled=True)  9.05 us
    convert_element_type x1, other arithmetic, layer_norm(): (centred * lax.rsqrt(spread + EPS) * gain + shift).astype(jnp.bfloat16)  8.79 us
    dot_general x1, matrix products, project(): jnp.dot(normed, weight.reshape(weight.shape[0], 3 * width), preferred_ele...  8.78 us
  transfers between devices with their start and end apart: 7, of which 3 were waited for; matrix products, arithmetic and copies ran while one was open for 27% of the time, Pallas kernels for 0%

commit v1 on v0

--- a/solution.py
+++ b/solution.py
@@ -160,8 +160,11 @@
     requests = decode_x.shape[0]
     rows = jnp.concatenate([prefill_x, decode_x], axis=0)
     partner = lax.ppermute(rows, "tz", [(0, 1), (1, 0)])
-    own_y = lax.all_gather(rows, "ty", axis=1, tiled=True)
-    partner_y = lax.all_gather(partner, "ty", axis=1, tiled=True)
+    own_y, partner_y = jnp.split(
+        lax.all_gather(jnp.concatenate([rows, partner], axis=0), "ty", axis=1, tiled=True),
+        [rows.shape[0]],
+        axis=0,
+    )
     lower = lax.axis_index("tz") == 0
     first = jnp.where(lower, own_y, partner_y).reshape(rows.shape[0], -1, 1, rows.shape[1])
     second = jnp.where(lower, partner_y, own_y).reshape(rows.shape[0], -1, 1, rows.shape[1])

time: 199 us -> 216 us (1.085)
  waiting for transfers between devices: 30.4 us -> 43.6 us
  local copies, waits for them, and re-layouts: 78.1 us -> 80.8 us
    all_gather x2 -> x1, waiting for transfers between devices: 9.05 us -> 22.5 us  [local(): lax.all_gather(jnp.concatenate([rows, partner], axis=0), 'ty', axis=1, ti...]
    concatenate x1, local copies, waits for them, and re-layouts: 0.7 us -> 7.37 us  [local(): jnp.concatenate([rows, partner], axis=0)]
    unnamed x24 -> x23, local copies, waits for them, and re-layouts: 12.5 us -> 9.84 us
  transfers between devices with their start and end apart: 7 -> 6, of which waited for: 3 -> 3; matrix products, arithmetic and copies ran while one was open for 27% -> 24% of each run, Pallas kernels for 0% -> 0%
where the time goes in v1:
time: 216 us; the launch traced here: 214 us
  local copies, waits for them, and re-layouts  80.8 us (37%)
  other arithmetic  44.1 us (20%)
  waiting for transfers between devices  43.6 us (20%)
  matrix products  17.1 us (8%)
  between operations  15.1 us (7%)
  starting transfers between devices  13.8 us (6%)
    all_gather x1, waiting for transfers between devices, local(): lax.all_gather(jnp.concatenate([rows, partner], axis=0), 'ty', axis=1, ti...  22.5 us
    reduce_sum x1, other arithmetic, layer_norm(): middle = jnp.mean(rows, axis=-1, keepdims=True)  14.9 us
    ppermute x1, waiting for transfers between devices, local(): partner = lax.ppermute(rows, 'tz', [(0, 1), (1, 0)])  14.4 us
    reshape x1, local copies, waits for them, and re-layouts, local(): jnp.where(lower, partner_y, own_y)  12.5 us
    convert_element_type x1, local copies, waits for them, and re-layouts, layer_norm(): (centred * lax.rsqrt(spread + EPS) * gain + shift).astype(jnp.bfloat16)  10.6 us
    unnamed x23, local copies, waits for them, and re-layouts  9.84 us
    convert_element_type x1, other arithmetic, layer_norm(): (centred * lax.rsqrt(spread + EPS) * gain + shift).astype(jnp.bfloat16)  8.78 us
    dot_general x1, matrix products, project(): jnp.dot(normed, weight.reshape(weight.shape[0], 3 * width), preferred_ele...  8.76 us
  transfers between devices with their start and end apart: 6, of which 3 were waited for; matrix products, arithmetic and copies ran while one was open for 24% of the time, Pallas kernels for 0%

profile of v1, /device:TPU:8, one launch (start us, length us, event | category | flops | bytes accessed | tf_op | source)
XLA Modules:
  0.0 214.4 jit_solution(18370113637261406508)
XLA Ops:
  7.2 1.1 pad_maximum_fusion.1
  8.3 7.3 %collective-permute-start = (bf16[516,512]{1,0:T(8,128)(2,1)S(1)}, bf16[516,512]{1,0:T(8,128)(2,1)S(1)}, u32[]{:S(2)}, u32[]{:S(2)}) collective-permute-start(bf16[516,512]{1,0:T(8,128)(2,1)S(1)} %pad_maximum_fusion.1), channel_id=1, source_target_pairs={{0,1},{1,0},{2,3},{3,2},{4,5},{5,4},{6,7},{7,6},{8,9},{9,8},{10,11... | collective-permute-start | bytes 1585160 | tf_op jit(solution)/shard_map/ppermute | solution.py:162
  15.6 14.4 %collective-permute-done = bf16[516,512]{1,0:T(8,128)(2,1)S(1)} collective-permute-done((bf16[516,512]{1,0:T(8,128)(2,1)S(1)}, bf16[516,512]{1,0:T(8,128)(2,1)S(1)}, u32[]{:S(2)}, u32[]{:S(2)}) %collective-permute-start) | collective-permute-done | bytes 528416 | tf_op jit(solution)/shard_map/ppermute | solution.py:162
  30.0 7.4 %concatenate.59 = bf16[1032,512]{1,0:T(8,128)(2,1)} concatenate(bf16[512,512]{1,0:T(8,128)(2,1)} %param.11, bf16[4,512]{1,0:T(4,128)(2,1)} %param.12, bf16[516,512]{1,0:T(8,128)(2,1)S(1)} %collective-permute-done), dimensions={0} | concatenate | bytes 2113536 | tf_op jit(solution)/shard_map/concatenate | solution.py:164
  37.4 8.8 %copy.95 = bf16[4096,3,256]{0,2,1:T(8,128)(2,1)} copy(bf16[4096,3,256]{2,0,1:T(8,128)(2,1)} %param.15) | data formatting | bytes 12582912 | tf_op args[4]
  46.9 0.2 slice_convert_fusion.7
  47.2 0.2 multiply_cosine_fusion
  47.4 0.1 copy.99
  47.5 0.8 copy.98
  48.4 0.1 copy.128
  48.6 0.8 copy.102
  49.4 0.8 copy.92
  50.3 5.7 %fusion.76 = (bf16[4,1,1024,256]{3,2,1,0:T(8,128)(2,1)S(1)}, bf16[4,1,1024,256]{3,2,1,0:T(8,128)(2,1)}, bf16[4,1,1024,256]{3,2,1,0:T(8,128)(2,1)}, bf16[4,1,1024,256]{3,2,1,0:T(8,128)(2,1)}) fusion(bf16[8,2,1024,256]{3,2,1,0:T(8,128)(2,1)} %param.21), kind=kLoop, calls=%fused_computation.135 | loop fusion | bytes 16777216 | tf_op jit(solution)/shard_map/slice | solution.py:118
  56.0 4.0 %copy.126 = bf16[4,1,1024,256]{2,3,0,1:T(8,128)(2,1)} copy(bf16[4,1,1024,256]{3,2,1,0:T(8,128)(2,1)} %get-tuple-element.43) | data formatting | bytes 4194304 | tf_op jit(solution)/shard_map/reshape;squeeze | solution.py:117
  60.0 4.1 %reshape_squeeze.30 = bf16[4,1024,2,128]{3,2,1,0:T(2,128)(2,1)} reshape(bf16[4,1,1024,256]{3,2,1,0:T(8,128)(2,1)} %get-tuple-element.42) | data formatting | bytes 4194304 | tf_op jit(solution)/shard_map/reshape;squeeze | solution.py:118
  64.0 2.1 fusion.78
  66.1 1.2 reshape_squeeze.31
  67.3 1.0 reshape_squeeze.28
  68.3 4.0 %copy.125 = bf16[4,1,1024,256]{2,3,0,1:T(8,128)(2,1)} copy(bf16[4,1,1024,256]{3,2,1,0:T(8,128)(2,1)} %get-tuple-element.41) | data formatting | bytes 4194304 | tf_op jit(solution)/shard_map/reshape;squeeze | solution.py:117
  72.3 2.1 reshape_squeeze.27
  74.6 1.0 pad_add_fusion
  75.6 22.5 %all-gather.2.cloned.1.call-done = bf16[1032,2048]{1,0:T(8,128)(2,1)} async-done(((bf16[1032,512]{1,0:T(8,128)(2,1)}), bf16[1032,2048]{1,0:T(8,128)(2,1)}) %all-gather.2.cloned.1.call-update) | async-done | bytes 4227088 | tf_op jit(solution)/shard_map/all_gather | solution.py:164
  98.0 4.2 %broadcast_select_fusion.1 = (bf16[516,2048]{1,0:T(8,128)(2,1)S(1)}, bf16[516,2048]{1,0:T(8,128)(2,1)}) fusion(pred[]{:T(512)S(6)} %eq.3, bf16[1032,2048]{1,0:T(8,128)(2,1)} %all-gather.2.cloned.1.call-done), kind=kLoop, calls=%fused_computation.14 | loop fusion | flops 2113536 | bytes 8454145 | tf_op jit(solution)/shard_map/jit(_where)/select_n | solution.py:169
  102.3 12.5 %reshape.299 = bf16[516,4,1,512]{3,2,1,0:T(2,128)(2,1)} reshape(bf16[516,2048]{1,0:T(8,128)(2,1)} %get-tuple-element.45) | data formatting | bytes 4227072 | tf_op jit(solution)/shard_map/reshape | solution.py:170
  114.8 5.5 %reshape.298 = bf16[516,4,1,512]{3,2,1,0:T(2,128)(2,1)} reshape(bf16[516,2048]{1,0:T(8,128)(2,1)S(1)} %get-tuple-element.44) | data formatting | bytes 4227072 | tf_op jit(solution)/shard_map/reshape | solution.py:169
  120.3 14.9 %convert_reduce_fusion = (f32[516]{0:T(1024)S(1)}, bf16[516,4,2,512]{3,2,1,0:T(2,128)(2,1)S(1)}) fusion(bf16[516,4,1,512]{3,2,1,0:T(2,128)(2,1)} %reshape.299, bf16[516,4,1,512]{3,2,1,0:T(2,128)(2,1)} %reshape.298), kind=kLoop, calls=%fused_computation.2 | loop fusion | flops 12680700 | bytes 8456208 | tf_op jit(solution)/shard_map/reduce_sum | solution.py:30
  135.1 6.1 %fusion.3 = f32[516]{0:T(1024)S(1)} fusion(bf16[516,4,2,512]{3,2,1,0:T(2,128)(2,1)S(1)} %get-tuple-element.39, f32[516]{0:T(1024)S(1)} %broadcast_multiply_fusion), kind=kLoop, calls=%fused_computation.5 | loop fusion | flops 8453628 | bytes 4231200 | tf_op jit(solution)/shard_map/reduce_sum | solution.py:32
  141.3 8.8 %fusion.6 = bf16[516,4,2,512]{3,2,1,0:T(2,128)(2,1)} fusion(bf16[516,4,2,512]{3,2,1,0:T(2,128)(2,1)S(1)} %get-tuple-element.39, f32[516]{0:T(1024)S(1)} %add_rsqrt_fusion, f32[516]{0:T(1024)S(1)} %broadcast_multiply_fusion, f32[4,2,512]{2,1,0:T(2,128)S(1)} %add.81, f32[4,2,512]{2,1,0:T(2,128)S(1)} %mul.188), kind=kLoop, calls=%fused_computation.8 | loop fusion | flops 12681216 | bytes 8491040 | tf_op jit(solution)/shard_map/convert_element_type | solution.py:33
  150.0 10.6 %convert_element_type.82 = bf16[516,4096]{1,0:T(8,128)(2,1)} reshape(bf16[516,4,2,512]{3,2,1,0:T(2,128)(2,1)} %fusion.6) | data formatting | bytes 8454144 | tf_op jit(solution)/shard_map/convert_element_type | solution.py:33
  160.6 8.8 %convolution_add_fusion = f32[516,768]{1,0:T(8,128)} fusion(bf16[516,4096]{1,0:T(8,128)(2,1)} %convert_element_type.82, bf16[4096,768]{0,1:T(8,128)(2,1)} %bitcast.118, f32[768]{0:T(1024)S(1)} %add.84), kind=kOutput, calls=%fused_computation.25 | convolution fusion | flops 3246787584 | bytes 12106752 | tf_op jit(solution)/shard_map/dot_general | solution.py:54
  169.4 2.1 reshape.279
  171.5 0.4 fusion.77
  171.8 2.2 %copy.96 = bf16[516,3,2,128]{0,3,2,1:T(8,128)(2,1)} copy(f32[516,3,2,128]{3,2,1,0:T(2,128)S(1)} %reshape.279) | data formatting | bytes 2377728 | tf_op jit(solution)/shard_map/reshape | solution.py:57
  174.1 0.1 slice.249
  174.3 0.1 slice.250
  174.4 1.4 subtract_convert_fusion.1
  175.9 0.3 pad_maximum_fusion.4
  176.2 1.0 slice_bitcast_fusion
  177.3 0.8 slice.182
  178.1 0.3 pad_maximum_fusion.5
  178.7 5.7 %collective-permute-start.1 = (f32[4,257]{1,0:T(4,128)S(1)}, f32[4,257]{1,0:T(4,128)S(1)}, u32[]{:S(2)}, u32[]{:S(2)}) collective-permute-start(f32[4,257]{1,0:T(4,128)S(1)} %get-tuple-element.68), channel_id=1, source_target_pairs={{8,0},{16,8},{24,16},{32,24},{40,32},{48,40},{56,48},{64,56},{72,6... | collective-permute-start | bytes 12344 | tf_op jit(solution)/shard_map/ppermute | solution.py:198
  184.4 0.7 fusion.33
  185.1 2.4 %fusion.80 = (f32[2,512]{1,0:T(2,128)S(1)}, bf16[2,512,1024]{2,1,0:T(8,128)(2,1)S(1)}) fusion(f32[2,512,1024]{2,1,0:T(8,128)S(1)} %fusion.33, pred[512,1024]{1,0:T(8,128)(4,1)S(1)} %copy-done.3), kind=kOutput, calls=%fused_computation.139 | output fusion | flops 8389631 | bytes 6819840 | tf_op jit(solution)/shard_map/while/body/eval_jaxpr/sub | solution.py:70
  187.5 0.7 pad_maximum_fusion.3
  188.2 0.7 pad_maximum_fusion.2
  188.9 0.3 fusion.28
  189.2 0.8 fusion.23
  190.1 0.2 fusion.56
  190.5 2.0 fusion.82
  192.5 0.2 fusion.50
  192.7 2.0 fusion.8
  194.7 0.2 copy.121
  195.0 0.2 collective-permute-start.4
  195.4 0.4 fusion.81
  195.9 0.2 fusion.51
  196.1 2.0 fusion.10
  198.1 0.2 copy.112
  198.3 0.4 collective-permute-start.2
  198.8 0.2 fusion.26
  199.0 0.9 copy.106
  199.8 0.2 copy.124
  200.0 6.7 %collective-permute-done.2 = f32[4,2,130]{0,1,2:T(2,128)S(1)} collective-permute-done((f32[4,2,130]{0,1,2:T(2,128)S(1)}, f32[4,2,130]{0,1,2:T(2,128)S(1)}, u32[]{:S(2)}, u32[]{:S(2)}) %collective-permute-start.2) | collective-permute-done | bytes 4192 | tf_op jit(solution)/shard_map/ppermute | solution.py:207
  206.8 0.1 fusion.41
  206.9 0.7 copy.105
  (62 shorter events, 1.7 us)
Async XLA Ops:
  7.2 30.2 %copy-start.7 = (f32[4096]{0:T(1024)S(1)}, f32[4096]{0:T(1024)}, u32[]{:S(2)}) copy-start(f32[4096]{0:T(1024)} %param.14) | copy-start | bytes 49156
  7.2 30.2 %copy-start.8 = (f32[4096]{0:T(1024)S(1)}, f32[4096]{0:T(1024)}, u32[]{:S(2)}) copy-start(f32[4096]{0:T(1024)} %param.13) | copy-start | bytes 49156
  7.2 90.8 %all-gather.2.cloned.1.call-start = ((), (), s32[]{:S(2)}) async-start(), calls=%async_computation | async-start | bytes 5283840 | tf_op jit(solution)/shard_map/all_gather | solution.py:164
  8.3 21.6 %collective-permute-start = (bf16[516,512]{1,0:T(8,128)(2,1)S(1)}, bf16[516,512]{1,0:T(8,128)(2,1)S(1)}, u32[]{:S(2)}, u32[]{:S(2)}) collective-permute-start(bf16[516,512]{1,0:T(8,128)(2,1)S(1)} %pad_maximum_fusion.1), channel_id=1, source_target_pairs={{0,1},{1,0},{2,3},{3,2},{4,5},{5,4},{6,7},{7,6},{8,9},{9,8},{10,11... | collective-permute-start | bytes 1585160 | tf_op jit(solution)/shard_map/ppermute | solution.py:162
  37.4 8.8 %copy-start.9 = (f32[3,256]{1,0:T(4,128)S(1)}, f32[3,256]{1,0:T(4,128)}, u32[]{:S(2)}) copy-start(f32[3,256]{1,0:T(4,128)} %param.16) | copy-start | bytes 9220
  37.4 9.5 %copy-start.6 = (s32[4,3]{1,0:T(4,128)S(1)}, s32[4,3]{1,0:T(4,128)}, u32[]{:S(2)}) copy-start(s32[4,3]{1,0:T(4,128)} %param.20) | copy-start | bytes 148
  37.4 11.0 %copy-start.4 = (bf16[1,2,512,256]{3,2,1,0:T(8,128)(2,1)S(1)}, bf16[1,2,512,256]{3,2,1,0:T(8,128)(2,1)}, u32[]{:S(2)}) copy-start(bf16[1,2,512,256]{3,2,1,0:T(8,128)(2,1)} %param.17) | copy-start | bytes 1572868
  174.4 10.0 %copy-start.2 = (bf16[512,2,128]{2,0,1:T(8,128)(2,1)S(1)}, bf16[512,2,128]{2,0,1:T(8,128)(2,1)}, u32[]{:S(2)}) copy-start(bf16[512,2,128]{2,0,1:T(8,128)(2,1)} %copy.102) | copy-start | bytes 786436
  176.2 8.9 %copy-start.3 = (pred[512,1024]{1,0:T(8,128)(4,1)S(1)}, pred[512,1024]{1,0:T(8,128)(4,1)}, u32[]{:S(2)}) copy-start(pred[512,1024]{1,0:T(8,128)(4,1)} %pad_add_fusion) | copy-start | bytes 1572868
  178.5 11.8 %collective-permute-start.3 = (f32[4,257]{1,0:T(4,128)S(1)}, f32[4,257]{1,0:T(4,128)S(1)}, u32[]{:S(2)}, u32[]{:S(2)}) collective-permute-start(f32[4,257]{1,0:T(4,128)S(1)} %get-tuple-element.69), channel_id=1, source_target_pairs={{0,8},{8,16},{16,24},{24,32},{32,40},{40,48},{48,56},{56,64},{64,7... | collective-permute-start | bytes 12344 | tf_op jit(solution)/shard_map/ppermute | solution.py:198
  178.7 16.5 %collective-permute-start.1 = (f32[4,257]{1,0:T(4,128)S(1)}, f32[4,257]{1,0:T(4,128)S(1)}, u32[]{:S(2)}, u32[]{:S(2)}) collective-permute-start(f32[4,257]{1,0:T(4,128)S(1)} %get-tuple-element.68), channel_id=1, source_target_pairs={{8,0},{16,8},{24,16},{32,24},{40,32},{48,40},{56,48},{64,56},{72,6... | collective-permute-start | bytes 12344 | tf_op jit(solution)/shard_map/ppermute | solution.py:198
  185.1 3.1 %copy-start.1 = (bf16[4,256,2,128]{3,2,1,0:T(2,128)(2,1)S(1)}, bf16[4,256,2,128]{3,2,1,0:T(2,128)(2,1)}, u32[]{:S(2)}) copy-start(bf16[4,256,2,128]{3,2,1,0:T(2,128)(2,1)} %reshape_squeeze.28) | copy-start | bytes 1572868
  185.1 4.1 %copy-start.5 = (bf16[1,1,512,256]{2,3,1,0:T(8,128)(2,1)S(1)}, bf16[1,1,512,256]{2,3,1,0:T(8,128)(2,1)}, u32[]{:S(2)}) copy-start(bf16[1,1,512,256]{2,3,1,0:T(8,128)(2,1)} %copy.92) | copy-start | bytes 786436
  189.2 6.2 %copy-start = (bf16[4,1,1024,256]{2,3,0,1:T(8,128)(2,1)S(1)}, bf16[4,1,1024,256]{2,3,0,1:T(8,128)(2,1)}, u32[]{:S(2)}) copy-start(bf16[4,1,1024,256]{2,3,0,1:T(8,128)(2,1)} %copy.125) | copy-start | bytes 6291460
  195.0 5.0 %collective-permute-start.4 = (f32[4,2,130]{0,1,2:T(2,128)S(1)}, f32[4,2,130]{0,1,2:T(2,128)S(1)}, u32[]{:S(2)}, u32[]{:S(2)}) collective-permute-start(f32[4,2,130]{0,1,2:T(2,128)S(1)} %pad_maximum_fusion.7), channel_id=1, source_target_pairs={{8,0},{16,8},{24,16},{32,24},{40,32},{48,40},{56,48},{64,56},{72,6... | collective-permute-start | bytes 12488 | tf_op jit(solution)/shard_map/ppermute | solution.py:207
  198.3 8.4 %collective-permute-start.2 = (f32[4,2,130]{0,1,2:T(2,128)S(1)}, f32[4,2,130]{0,1,2:T(2,128)S(1)}, u32[]{:S(2)}, u32[]{:S(2)}) collective-permute-start(f32[4,2,130]{0,1,2:T(2,128)S(1)} %pad_maximum_fusion.6), channel_id=1, source_target_pairs={{0,8},{8,16},{16,24},{24,32},{32,40},{40,48},{48,56},{56,64},{64,7... | collective-permute-start | bytes 12488 | tf_op jit(solution)/shard_map/ppermute | solution.py:207
Sparse Core Ops, SparseCore 0:
  37.5 60.5 all-gather.1
